TPU v7x, 512 devices: a whole 4x8x8 slice. The times are simulated.
512 devices in a mesh: grp: 64 (over z_hi, y, core), mdl: 8 (over z_lo, x).
Axes of the slice: x: 4, y: 8, z: 8 (z_hi: 4, z_lo: 2; z = z_hi * 2 + z_lo), core: 2. Of those that a mesh axis runs over, the one named last changes fastest.
Arguments:
- draft_hidden: bfloat16 [128, 32, 2048], P('grp', None, 'mdl'), may hold values from -6 to 6
- q_weight: bfloat16 [4, 2048, 1024], P(None, None, 'mdl'), may hold values from -0.125 to 0.125
- kv_weight: bfloat16 [2, 2048, 1024], P(None, None, 'mdl'), may hold values from -0.125 to 0.125
- router_weight: float32 [2048, 4], replicated, may hold values from -0.125 to 0.125
- routes: int32 [128, 32, 2], P('grp'), may hold values from 0 to 3, all different within a row
- tree_mask: int32 [128, 32, 32], P('grp'), may hold values from 0 to 1, as said below
- accepted: int32 [128, 8], P('grp'), may hold values from 0 to 31, as said below
- cache_kv: bfloat16 [192, 2, 1024, 1024], P('grp', None, None, 'mdl')
- cache_len: int32 [192], P('grp'), may hold values from 1 to 1024
- slot_request: int32 [192], replicated, may hold values from 0 to 127, as said below
Outputs:
- verified: bfloat16 [128, 8, 2, 1024], P('grp', None, None, 'mdl')
Inputs may be any that keep to these rules, and one draw needn't show every extreme that they name: `routes`: the 2 experts of one token differ. tree_mask[r, i, j] is 1 exactly when draft j is draft i or an ancestor of it; every draft's parent has a lower index and draft 0 is the root. `accepted`: each row holds the first 8 drafts of the root-to-node chain of one draft, in increasing order; a shorter chain is followed by repeats of its last draft. `slot_request`: the requests of one index of grp are the 2 in a row that it holds; they are served by 3 slots in all, 1 of them by two slots and the others by one; no index of grp holds more than 1 slot serving requests of any one index of grp, and some pairs of indices have exactly 1 such slot.
All inputs are finite; a program needn't handle non-finite values.
Results may differ from a plain program's by a relative error of at most 0.014.
The roundings to bfloat16 on the way count: a program that leaves them out, or rounds other values in their place, can miss the bound.
Values may be sent and summed in bfloat16 or wider, within the bound.
No kernel may reach another device: no remote copies, remote signals or barrier semaphores. Data moves between devices by JAX's collectives and lax.ppermute only.
A program may use at most 64 MiB of HBM per device.

v0:
```python
import jax
import jax.numpy as jnp
from jax import lax
from jax.sharding import PartitionSpec as P

HEAD_SIZE = 128


def softmax_piece(scores, usable, values, contract):
    masked = jnp.where(usable, scores, -jnp.inf)
    peak_score = jnp.max(masked, axis=-1)
    weights_low = jnp.exp(masked - peak_score[..., None]).astype(jnp.bfloat16)
    denominator = jnp.sum(weights_low.astype(jnp.float32), axis=-1)
    numerator = jnp.einsum(contract, weights_low, values, preferred_element_type=jnp.float32)
    return (peak_score, denominator, numerator)


def blend(running, pieces, matched):
    running_max, denominator, numerator = running
    piece_peak, piece_den, piece_num = pieces
    candidate = jnp.where(matched[:, :, None, None, None], piece_peak[None], -jnp.inf)
    new_max = jnp.maximum(running_max, jnp.max(candidate, axis=1))
    rescale = jnp.exp(running_max - new_max)
    weight = jnp.exp(candidate - new_max[:, None])
    denominator = denominator * rescale + jnp.sum(weight * piece_den[None], axis=1)
    numerator = numerator * rescale[..., None] + jnp.einsum(
        "rnqkh,nqkhd->rqkhd", weight, piece_num, precision=lax.Precision.HIGHEST
    )
    return (new_max, denominator, numerator)


def on_device(
    draft_hidden,
    q_weight,
    kv_weight,
    router_weight,
    routes,
    tree_mask,
    accepted,
    cache_kv,
    cache_len,
    slot_request,
):
    highest = lax.Precision.HIGHEST
    requests, drafts, part_width = draft_hidden.shape
    experts = q_weight.shape[0]
    head_width = q_weight.shape[2]
    head_count = head_width // HEAD_SIZE
    topk_count = routes.shape[2]
    row_count = requests * drafts
    score_scale = HEAD_SIZE ** (-0.5)
    pieces = lax.all_gather(draft_hidden, "mdl", axis=2, tiled=True)
    piece_size = pieces.shape[2]
    piece_rows = pieces.reshape(row_count, piece_size)
    q_sum = jnp.einsum("nd,edw->new", piece_rows, q_weight, preferred_element_type=jnp.float32)
    kv_sum = jnp.einsum("nd,cdw->ncw", piece_rows, kv_weight, preferred_element_type=jnp.float32)
    logit_sum = jnp.dot(piece_rows.astype(jnp.float32), router_weight, precision=highest)
    route_flat = routes.reshape(row_count, topk_count)
    chosen_mask = route_flat[:, :, None] == jnp.arange(experts, dtype=jnp.int32)[None, None, :]
    chosen = jnp.sum(jnp.where(chosen_mask, logit_sum[:, None, :], 0.0), axis=2)
    gate_probs = jax.nn.softmax(chosen, axis=-1).reshape(requests, drafts, topk_count)
    queries = jnp.sum(jnp.where(chosen_mask[:, :, :, None], q_sum[:, None], 0.0), axis=2)
    queries = queries.astype(jnp.bfloat16).reshape(
        requests, drafts, topk_count, head_count, HEAD_SIZE
    )
    draft_keys = kv_sum[:, 0].astype(jnp.bfloat16).reshape(requests, drafts, head_count, HEAD_SIZE)
    draft_values = (
        kv_sum[:, 1].astype(jnp.bfloat16).reshape(requests, drafts, head_count, HEAD_SIZE)
    )
    query_len = queries.shape[1]
    tree_scores = (
        jnp.einsum("rqkhd,rjhd->rqkhj", queries, draft_keys, preferred_element_type=jnp.float32)
        * score_scale
    )
    allowed = (tree_mask > 0)[:, :, None, None, :]
    tree_peak, tree_den, tree_num = softmax_piece(
        tree_scores, allowed, draft_values, "rqkhj,rjhd->rqkhd"
    )
    slot_count = cache_kv.shape[0]
    cache_size = cache_kv.shape[2]
    group_idx = lax.axis_index("grp")
    sending = queries.reshape(requests, query_len, topk_count * head_width)
    my_requests = lax.dynamic_slice_in_dim(slot_request, group_idx * slot_count, slot_count)
    pieces = lax.all_gather(sending, "grp", axis=0, tiled=True)
    piece_count = pieces.shape[0]
    selector = (my_requests[:, None] == jnp.arange(piece_count, dtype=jnp.int32)[None, :]).astype(
        jnp.bfloat16
    )
    slot_queries = jnp.einsum(
        "sn,nqw->sqw", selector, pieces, preferred_element_type=jnp.float32
    ).astype(jnp.bfloat16)
    slot_queries = slot_queries.reshape(slot_count, query_len, topk_count, head_count, HEAD_SIZE)
    cache_keys = cache_kv[:, 0].reshape(slot_count, cache_size, head_count, HEAD_SIZE)
    cache_values = cache_kv[:, 1].reshape(slot_count, cache_size, head_count, HEAD_SIZE)
    slot_scores = (
        jnp.einsum(
            "sqkhd,schd->sqkhc", slot_queries, cache_keys, preferred_element_type=jnp.float32
        )
        * score_scale
    )
    in_cache = (jnp.arange(cache_size, dtype=jnp.int32)[None, :] < cache_len[:, None])[
        :, None, None, None, :
    ]
    slot_peak, slot_den, slot_num = softmax_piece(
        slot_scores, in_cache, cache_values, "sqkhc,schd->sqkhd"
    )
    home_ids = group_idx * requests + jnp.arange(requests, dtype=jnp.int32)
    pieces = (
        lax.all_gather(slot_peak, "grp", axis=0, tiled=True),
        lax.all_gather(slot_den, "grp", axis=0, tiled=True),
        lax.all_gather(slot_num, "grp", axis=0, tiled=True),
    )
    running_max, denominator, numerator = blend(
        (tree_peak, tree_den, tree_num), pieces, home_ids[:, None] == slot_request[None, :]
    )
    final_num = jnp.take_along_axis(numerator, accepted[:, :, None, None, None], axis=1)
    final_den = jnp.take_along_axis(denominator, accepted[:, :, None, None], axis=1)
    final_gate = jnp.take_along_axis(gate_probs, accepted[:, :, None], axis=1)
    mixed = final_gate[:, :, :, None, None] * final_num / final_den[..., None]
    kept_rows = accepted.shape[1]
    return mixed.reshape(requests, kept_rows, topk_count, head_width).astype(jnp.bfloat16)


def solution(mesh):
    in_specs = (
        P("grp", None, "mdl"),
        P(None, None, "mdl"),
        P(None, None, "mdl"),
        P(),
        P("grp", None, None),
        P("grp", None, None),
        P("grp", None),
        P("grp", None, None, "mdl"),
        P("grp"),
        P(),
    )
    out_specs = P("grp", None, None, "mdl")
    return jax.shard_map(
        on_device, mesh=mesh, in_specs=in_specs, out_specs=out_specs, check_vma=False
    )
```

profile of v0, /device:TPU:1, one launch (start us, length us, event | category | flops | bytes accessed | tf_op | source)
XLA Modules:
  0.0 317.8 jit_solution(7277483683072777976)
XLA Ops:
  6.5 0.8 copy.87
  7.5 24.4 %all_gather.15 = bf16[2,32,2048]{2,1,0:T(8,128)(2,1)S(1)} all-gather(bf16[2,32,256]{2,1,0:T(8,128)(2,1)} %param.10), channel_id=1, replica_groups=mesh['grp'=64,'mdl'=8] {'mdl'}, dimensions={2}, use_global_device_ids=true | all-gather | bytes 294912 | tf_op jit(solution)/shard_map/all_gather | solution.py:52
  31.9 0.5 fusion.48
  32.4 0.1 select_reduce_fusion
  32.6 0.6 convert_element_type.49
  33.4 94.7 %all-gather.5.cloned.1.call-done = bf16[128,32,256]{2,1,0:T(8,128)(2,1)} async-done(((bf16[2,32,256]{2,1,0:T(8,128)(2,1)}), bf16[128,32,256]{2,1,0:T(8,128)(2,1)}) %all-gather.5.cloned.1.call-update) | async-done | bytes 2097168 | tf_op jit(solution)/shard_map/all_gather | solution.py:84
  128.1 2.8 fusion.8
  131.0 1.6 fusion.45
  132.6 2.1 convolution_bitcast_fusion
  134.9 0.3 fusion.47
  135.7 0.6 gather_fusion
  136.4 1.5 convolution_convert_fusion
  138.0 0.2 fusion.46
  138.3 80.5 %all-gather = f32[192,32,2]{1,2,0:T(2,128)S(1)} all-gather(f32[3,32,2]{1,2,0:T(2,128)S(1)} %get-tuple-element.11), channel_id=2, replica_groups=mesh['grp'=64,'mdl'=8] {'grp'}, dimensions={0}, use_global_device_ids=true | all-gather | bytes 49920 | tf_op jit(solution)/shard_map/all_gather | solution.py:109
  218.9 0.1 copy.103
  219.2 0.3 convert_reduce_fusion
  219.5 77.0 %all-gather.1 = f32[192,32,2]{1,2,0:T(2,128)S(1)} all-gather(f32[3,32,2]{1,2,0:T(2,128)S(1)} %convert_reduce_fusion), channel_id=3, replica_groups=mesh['grp'=64,'mdl'=8] {'grp'}, dimensions={0}, use_global_device_ids=true | all-gather | bytes 49920 | tf_op jit(solution)/shard_map/all_gather | solution.py:110
  296.5 0.1 copy.107
  296.6 0.2 fusion.24
  296.9 0.6 gather_fusion.2
  297.8 11.6 %fusion = f32[32,2,128,2]{2,3,1,0:T(2,128)S(1)} fusion(f32[192,32,2,1,128]{4,1,3,2,0:T(8,128)} %all-gather.7.cloned.1.call-done, pred[2,192]{1,0:T(4,128)(4,1)S(1)} %broadcast_compare_fusion.1, f32[2,32,2]{0,2,1:T(2,128)S(1)} %copy.104, f32[192,32,2]{0,2,1:T(2,128)S(1)} %copy.103), kind=kOutput, calls=%fused_computation.3 | convolution fusion | flops 37797888 | bytes 6407040 | tf_op jit(solution)/shard_map/rnqkh,nqkhd->rqkhd/dot_general | solution.py:26
  309.4 0.2 fusion.14
  309.6 0.6 gather_fusion.1
  310.3 0.7 fusion.35
  (51 shorter events, 2.0 us)
Async XLA Ops:
  6.5 25.4 %copy-start = (bf16[4,2048,128]{2,1,0:T(8,128)(2,1)S(1)}, bf16[4,2048,128]{2,1,0:T(8,128)(2,1)}, u32[]{:S(2)}) copy-start(bf16[4,2048,128]{2,1,0:T(8,128)(2,1)} %param.11) | copy-start | bytes 6291460
  6.5 26.7 %copy-start.4 = (s32[192]{0:T(256)S(1)}, s32[192]{0:T(256)}, u32[]{:S(2)}) copy-start(s32[192]{0:T(256)} %param.19) | copy-start | bytes 2308
  6.5 26.8 %copy-start.5 = (s32[3]{0:T(128)S(1)}, s32[3]{0:T(128)}, u32[]{:S(2)}) copy-start(s32[3]{0:T(128)} %param.18) | copy-start | bytes 40
  6.5 121.6 %all-gather.5.cloned.1.call-start = ((), (), s32[]{:S(2)}) async-start(), calls=%async_computation | async-start | bytes 2129920 | tf_op jit(solution)/shard_map/all_gather | solution.py:84
  33.2 264.6 %all-gather.7.cloned.1.call-start = ((), (), s32[]{:S(2)}) async-start(), calls=%async_computation.1 | async-start | bytes 6389760 | tf_op jit(solution)/shard_map/all_gather | solution.py:111
  130.9 3.8 %copy-start.3 = (s32[2,8]{1,0:T(2,128)S(1)}, s32[2,8]{1,0:T(2,128)}, u32[]{:S(2)}) copy-start(s32[2,8]{1,0:T(2,128)} %param.16) | copy-start | bytes 196
  130.9 3.9 %copy-start.2 = (s32[2,32,32]{2,1,0:T(8,128)S(1)}, s32[2,32,32]{2,1,0:T(8,128)}, u32[]{:S(2)}) copy-start(s32[2,32,32]{2,1,0:T(8,128)} %param.15) | copy-start | bytes 24580
  130.9 4.0 %copy-start.1 = (f32[2048,4]{0,1:T(4,128)S(1)}, f32[2048,4]{0,1:T(4,128)}, u32[]{:S(2)}) copy-start(f32[2048,4]{0,1:T(4,128)} %param.13) | copy-start | bytes 98308
Sparse Core Ops, SparseCore 0:
  33.3 94.7 all-gather.4
  134.8 91.8 all-gather.6
where the time goes:
time: 318 us
  blocking collectives  182 us (57%)
  waiting for transfers between devices  94.7 us (30%)
  matrix products  20.8 us (7%)
  between operations  13.6 us (4%)
  local copies, waits for them, and re-layouts  4.98 us (2%)
    all_gather x1, waiting for transfers between devices, on_device(): pieces = lax.all_gather(sending, 'grp', axis=0, tiled=True)  94.7 us
    all_gather x1, blocking collectives, on_device(): lax.all_gather(slot_peak, 'grp', axis=0, tiled=True)  80.5 us
    all_gather x1, blocking collectives, on_device(): lax.all_gather(slot_den, 'grp', axis=0, tiled=True)  77 us
    all_gather x1, blocking collectives, on_device(): pieces = lax.all_gather(draft_hidden, 'mdl', axis=2, tiled=True)  24.4 us
    dot_general x1, matrix products, blend(): jnp.einsum('rnqkh,nqkhd->rqkhd', weight, piece_num, precision=lax.Precisi...  11.6 us
  transfers between devices with their start and end apart: 2, of which 1 were waited for; matrix products, arithmetic and copies ran while one was open for 2% of the time, Pallas kernels for 0%

commit v1 on v0

--- a/solution.py
+++ b/solution.py
@@ -4,6 +4,13 @@
 from jax.sharding import PartitionSpec as P
 
 HEAD_SIZE = 128
+
+
+def exchange_gather(x, mesh_axis, dim):
+    count = lax.axis_size(mesh_axis)
+    blocks = jnp.stack([x for _ in range(count)])
+    blocks = lax.all_to_all(blocks, mesh_axis, split_axis=0, concat_axis=0)
+    return jnp.concatenate(blocks, axis=dim)
 
 
 def softmax_piece(scores, usable, values, contract):
@@ -81,7 +88,7 @@
     group_idx = lax.axis_index("grp")
     sending = queries.reshape(requests, query_len, topk_count * head_width)
     my_requests = lax.dynamic_slice_in_dim(slot_request, group_idx * slot_count, slot_count)
-    pieces = lax.all_gather(sending, "grp", axis=0, tiled=True)
+    pieces = exchange_gather(sending, "grp", 0)
     piece_count = pieces.shape[0]
     selector = (my_requests[:, None] == jnp.arange(piece_count, dtype=jnp.int32)[None, :]).astype(
         jnp.bfloat16

time: 318 us -> 309 us (0.972)
  waiting for transfers between devices: 94.7 us -> 52.5 us
  starting transfers between devices: 0.04 us -> 22.5 us
  local copies, waits for them, and re-layouts: 4.98 us -> 16.9 us
    all_gather x1 -> x0, waiting for transfers between devices: 94.7 us -> none  [on_device(): pieces = lax.all_gather(sending, 'grp', axis=0, tiled=True)]
    all_to_all x0 -> x1, waiting for transfers between devices: none -> 52.5 us  [exchange_gather(): blocks = lax.all_to_all(blocks, mesh_axis, split_axis=0, concat_axis=0)]
    all_to_all x0 -> x1, starting transfers between devices: none -> 22.5 us  [exchange_gather(): blocks = lax.all_to_all(blocks, mesh_axis, split_axis=0, concat_axis=0)]
    all_to_all x0 -> x1, local copies, waits for them, and re-layouts: none -> 5.06 us  [exchange_gather(): blocks = lax.all_to_all(blocks, mesh_axis, split_axis=0, concat_axis=0)]
    reshape x0 -> x1, local copies, waits for them, and re-layouts: none -> 4.11 us  [exchange_gather(): return jnp.concatenate(blocks, axis=dim)]
    another operation x1 -> x2, local copies, waits for them, and re-layouts: 0.05 us -> 3.37 us  [the longest x1 3.32 us: exchange_gather(): blocks = jnp.stack([x for _ in range(count)])]
where the time goes in v1:
time: 309 us; the launch traced here: 308 us
  blocking collectives  181 us (59%)
  waiting for transfers between devices  52.5 us (17%)
  starting transfers between devices  22.5 us (7%)
  matrix products  20 us (6%)
  local copies, waits for them, and re-layouts  16.9 us (5%)
  between operations  13.6 us (4%)
    all_gather x1, blocking collectives, on_device(): lax.all_gather(slot_peak, 'grp', axis=0, tiled=True)  79.4 us
    all_gather x1, blocking collectives, on_device(): lax.all_gather(slot_den, 'grp', axis=0, tiled=True)  77.2 us
    all_to_all x1, waiting for transfers between devices, exchange_gather(): blocks = lax.all_to_all(blocks, mesh_axis, split_axis=0, concat_axis=0)  52.5 us
    all_gather x1, blocking collectives, on_device(): pieces = lax.all_gather(draft_hidden, 'mdl', axis=2, tiled=True)  24.4 us
    all_to_all x1, starting transfers between devices, exchange_gather(): blocks = lax.all_to_all(blocks, mesh_axis, split_axis=0, concat_axis=0)  22.5 us
    dot_general x1, matrix products, blend(): jnp.einsum('rnqkh,nqkhd->rqkhd', weight, piece_num, precision=lax.Precisi...  11.6 us
  transfers between devices with their start and end apart: 2, of which 1 were waited for; matrix products, arithmetic and copies ran while one was open for 2% of the time, Pallas kernels for 0%

profile of v1, /device:TPU:1, one launch (start us, length us, event | category | flops | bytes accessed | tf_op | source)
XLA Modules:
  0.0 308.3 jit_solution(5158137381475810154)
XLA Ops:
  6.5 0.8 copy.88
  7.5 24.4 %all_gather.12 = bf16[2,32,2048]{2,1,0:T(8,128)(2,1)S(1)} all-gather(bf16[2,32,256]{2,1,0:T(8,128)(2,1)} %param.10), channel_id=1, replica_groups=mesh['grp'=64,'mdl'=8] {'mdl'}, dimensions={2}, use_global_device_ids=true | all-gather | bytes 294912 | tf_op jit(solution)/shard_map/all_gather | solution.py:59
  31.9 0.5 fusion.43
  32.6 3.3 %stack.3 = bf16[64,2,32,256]{3,1,2,0:T(2,128)(2,1)} broadcast(bf16[2,32,256]{2,0,1:T(2,128)(2,1)S(1)} %copy.96), dimensions={1,2,3} | broadcast | bytes 2129920 | tf_op jit(solution)/shard_map/stack | solution.py:11
  36.0 22.5 %all-to-all-start = ((bf16[64,2,32,256]{3,1,2,0:T(2,128)(2,1)}), bf16[64,2,32,256]{3,1,2,0:T(2,128)(2,1)}, u32[]{:S(2)}, u32[]{:S(2)}) async-start(bf16[64,2,32,256]{3,1,2,0:T(2,128)(2,1)} %stack.3), calls=%async_computation | async-start | bytes 4194304 | tf_op jit(solution)/shard_map/all_to_all | solution.py:12
  58.7 52.5 %all-to-all-done = bf16[64,2,32,256]{3,1,2,0:T(2,128)(2,1)} async-done(((bf16[64,2,32,256]{3,1,2,0:T(2,128)(2,1)}), bf16[64,2,32,256]{3,1,2,0:T(2,128)(2,1)}, u32[]{:S(2)}, u32[]{:S(2)}) %all-to-all-start) | async-done | bytes 2097184 | tf_op jit(solution)/shard_map/all_to_all | solution.py:12
  111.2 5.1 %copy.97 = bf16[64,2,32,256]{3,1,0,2:T(2,128)(2,1)} copy(bf16[64,2,32,256]{3,1,2,0:T(2,128)(2,1)} %all-to-all-done) | data formatting | bytes 4194304 | tf_op jit(solution)/shard_map/all_to_all | solution.py:12
  116.2 4.1 %reshape.291 = bf16[128,32,256]{2,0,1:T(8,128)(2,1)} reshape(bf16[64,2,32,256]{3,1,0,2:T(2,128)(2,1)} %copy.97) | data formatting | bytes 4194304 | tf_op jit(solution)/shard_map/reshape | solution.py:13
  120.4 2.0 convolution_convert_fusion
  122.4 1.6 fusion.40
  124.1 2.1 convolution_bitcast_fusion
  126.4 0.3 fusion.42
  127.2 0.6 gather_fusion
  127.9 1.5 convolution_convert_fusion.1
  129.4 0.2 fusion.41
  129.7 79.4 %all-gather = f32[192,32,2]{1,2,0:T(2,128)S(1)} all-gather(f32[3,32,2]{1,2,0:T(2,128)S(1)} %get-tuple-element.11), channel_id=2, replica_groups=mesh['grp'=64,'mdl'=8] {'grp'}, dimensions={0}, use_global_device_ids=true | all-gather | bytes 49920 | tf_op jit(solution)/shard_map/all_gather | solution.py:116
  209.6 0.3 convert_reduce_fusion
  209.8 77.2 %all-gather.1 = f32[192,32,2]{1,2,0:T(2,128)S(1)} all-gather(f32[3,32,2]{1,2,0:T(2,128)S(1)} %convert_reduce_fusion), channel_id=3, replica_groups=mesh['grp'=64,'mdl'=8] {'grp'}, dimensions={0}, use_global_device_ids=true | all-gather | bytes 49920 | tf_op jit(solution)/shard_map/all_gather | solution.py:117
  287.1 0.2 fusion.19
  287.4 0.6 gather_fusion.2
  288.3 11.6 %fusion = f32[32,2,128,2]{2,3,1,0:T(2,128)S(1)} fusion(f32[192,32,2,1,128]{4,1,3,2,0:T(8,128)} %all-gather.4.cloned.1.call-done, pred[2,192]{1,0:T(4,128)(4,1)S(1)} %broadcast_compare_fusion.1, f32[2,32,2]{0,2,1:T(2,128)S(1)} %copy.106, f32[192,32,2]{0,2,1:T(2,128)S(1)} %copy.105), kind=kOutput, calls=%fused_computation.3 | convolution fusion | flops 37797888 | bytes 6407040 | tf_op jit(solution)/shard_map/rnqkh,nqkhd->rqkhd/dot_general | solution.py:33
  299.9 0.2 fusion.9
  300.2 0.6 gather_fusion.1
  300.8 0.7 fusion.30
  (54 shorter events, 2.4 us)
Async XLA Ops:
  6.5 25.4 %copy-start = (bf16[4,2048,128]{2,1,0:T(8,128)(2,1)S(1)}, bf16[4,2048,128]{2,1,0:T(8,128)(2,1)}, u32[]{:S(2)}) copy-start(bf16[4,2048,128]{2,1,0:T(8,128)(2,1)} %param.11) | copy-start | bytes 6291460
  36.0 22.5 %copy-start.4 = (s32[192]{0:T(256)S(1)}, s32[192]{0:T(256)}, u32[]{:S(2)}) copy-start(s32[192]{0:T(256)} %param.19) | copy-start | bytes 2308
  36.0 22.6 %copy-start.5 = (s32[3]{0:T(128)S(1)}, s32[3]{0:T(128)}, u32[]{:S(2)}) copy-start(s32[3]{0:T(128)} %param.18) | copy-start | bytes 40
  36.0 75.2 %all-to-all-start = ((bf16[64,2,32,256]{3,1,2,0:T(2,128)(2,1)}), bf16[64,2,32,256]{3,1,2,0:T(2,128)(2,1)}, u32[]{:S(2)}, u32[]{:S(2)}) async-start(bf16[64,2,32,256]{3,1,2,0:T(2,128)(2,1)} %stack.3), calls=%async_computation | async-start | bytes 4194304 | tf_op jit(solution)/shard_map/all_to_all | solution.py:12
  58.4 229.9 %all-gather.4.cloned.1.call-start = ((), (), s32[]{:S(2)}) async-start(), calls=%async_computation.1 | async-start | bytes 6389760 | tf_op jit(solution)/shard_map/all_gather | solution.py:118
  122.4 3.8 %copy-start.3 = (s32[2,8]{1,0:T(2,128)S(1)}, s32[2,8]{1,0:T(2,128)}, u32[]{:S(2)}) copy-start(s32[2,8]{1,0:T(2,128)} %param.16) | copy-start | bytes 196
  122.4 3.9 %copy-start.2 = (s32[2,32,32]{2,1,0:T(8,128)S(1)}, s32[2,32,32]{2,1,0:T(8,128)}, u32[]{:S(2)}) copy-start(s32[2,32,32]{2,1,0:T(8,128)} %param.15) | copy-start | bytes 24580
  122.4 4.0 %copy-start.1 = (f32[2048,4]{0,1:T(4,128)S(1)}, f32[2048,4]{0,1:T(4,128)}, u32[]{:S(2)}) copy-start(f32[2048,4]{0,1:T(4,128)} %param.13) | copy-start | bytes 98308
Sparse Core Ops, SparseCore 0:
  126.3 98.3 all-gather.3
